TPU v7x, 256 devices: a whole 4x4x8 slice. The times are simulated.
256 devices in a mesh: row: 8 (over y, core), col: 32 (over x, z).
Axes of the slice: x: 4, y: 4, z: 8, core: 2. Of those that a mesh axis runs over, the one named last changes fastest.
Arguments:
- hidden: bfloat16 [32768, 4608], P('col', 'row'), may hold values from -6 to 6
- w_query: bfloat16 [4608, 4096], P('col', 'row'), may hold values from -0.09375 to 0.09375
- w_key: bfloat16 [4608, 2048], P('col', 'row'), may hold values from -0.09375 to 0.09375
- w_value: bfloat16 [4608, 2048], P('col', 'row'), may hold values from -0.09375 to 0.09375
- adapter_down: bfloat16 [32, 4608, 32], P('col', 'row'), may hold values from -0.09375 to 0.09375
- adapter_up_query: bfloat16 [32, 16, 4096], P('col', None, 'row'), may hold values from -1.5 to 1.5
- adapter_up_value: bfloat16 [32, 16, 2048], P('col', None, 'row'), may hold values from -1.5 to 1.5
- lengths: int32 [32, 10], P('col'), may hold values from 1 to 192, 1024 in all within a row
- request_adapter: int32 [32, 10], P('col'), may hold values from 0 to 31
- adapter_slot: int32 [32], replicated, may hold values from 0 to 31, each once
- page_table: int32 [32, 18], P('col'), may hold values from 0 to 17, each once within a row
Outputs:
- query: bfloat16 [32768, 4096], P('col', 'row')
- key_cache: bfloat16 [576, 128, 2048], P('col', None, 'row')
- value_cache: bfloat16 [576, 128, 2048], P('col', None, 'row')
Inputs may be any that keep to these rules, and one draw needn't show every extreme that they name: Each row of lengths sums to 1024, and its longest request has exactly 192 tokens. `adapter_slot`: a permutation of the slots. `page_table`: each row is a permutation of the 18 local slots.
All inputs are finite; a program needn't handle non-finite values.
Results may differ from a plain program's by a relative error of at most 0.0039.
Values may be sent and summed in bfloat16 or wider, within the bound.
No kernel may reach another device: no remote copies, remote signals or barrier semaphores. Data moves between devices by JAX's collectives and lax.ppermute only.
A program may use at most 128 MiB of HBM per device.

v0:
```python
import math
import jax
import jax.numpy as jnp
from jax import lax
from jax.sharding import PartitionSpec as P

HEAD = 128
PAGE = 128
TOK_DEV = 1024


def rotate(values, cosine, sine_value):
    half_width = HEAD // 2
    shaped = values.reshape(values.shape[0], -1, HEAD)
    leading = shaped[:, :, :half_width]
    second = shaped[:, :, half_width:]
    rotated = jnp.concatenate(
        [leading * cosine - second * sine_value, second * cosine + leading * sine_value], axis=2
    )
    return rotated.reshape(values.shape)


def token_layout(lengths, chosen_request):
    token_index = jnp.arange(TOK_DEV, dtype=jnp.int32)
    starts = jnp.cumsum(lengths) - lengths
    inside = (token_index[:, None] >= starts[None, :]) & (
        token_index[:, None] < (starts + lengths)[None, :]
    )
    inside = inside.astype(jnp.int32)
    position = token_index - jnp.sum(inside * starts[None, :], axis=1)
    chosen = jnp.sum(inside * chosen_request[None, :], axis=1)
    return (starts, position, chosen)


def cache_rows(lengths, starts, page_row):
    pages = page_row.shape[0]
    pages_each = (lengths + PAGE - 1) // PAGE
    page_start = jnp.cumsum(pages_each) - pages_each
    page_ids = jnp.arange(pages, dtype=jnp.int32)
    owner = (page_row[:, None] == page_ids[None, :]).astype(jnp.int32)
    page_of_slot = jnp.sum(owner * page_ids[:, None], axis=0)
    member = (page_of_slot[:, None] >= page_start[None, :]) & (
        page_of_slot[:, None] < (page_start + pages_each)[None, :]
    )
    member = member.astype(jnp.int32)
    used = jnp.sum(member, axis=1) > 0
    first_page = jnp.sum(member * page_start[None, :], axis=1)
    first_token = jnp.sum(member * starts[None, :], axis=1)
    length = jnp.sum(member * lengths[None, :], axis=1)
    offset = (page_of_slot - first_page) * PAGE
    source = first_token + offset
    valid = jnp.where(used, jnp.minimum(length - offset, PAGE), 0)
    inner = jnp.arange(PAGE, dtype=jnp.int32)
    rows = (source[:, None] + inner[None, :]).reshape(-1)
    keep = (inner[None, :] < valid[:, None]).reshape(-1)
    rows = jnp.clip(rows, 0, TOK_DEV - 1)
    return (rows, keep)


def shards(
    hidden,
    w_query,
    w_key,
    w_value,
    adapter_down,
    adapter_up_query,
    adapter_up_value,
    lengths,
    request_adapter,
    adapter_slot,
    page_table,
):
    lengths = lengths[0]
    chosen_request = jnp.take(adapter_slot, request_adapter[0])
    starts, position, chosen = token_layout(lengths, chosen_request)
    adapter_count = adapter_slot.shape[0]
    rank_width = adapter_up_query.shape[1]
    query_width = w_query.shape[1]
    key_width = w_key.shape[1]
    weight_width = query_width + 2 * key_width
    feature_rows = w_query.shape[0]
    down_shape = adapter_down.shape[1:]
    row_size = lax.axis_size("row")
    with jax.named_scope("gathers"):
        full_rows = lax.all_gather(hidden, "row", axis=1, tiled=True)
        pieces = [
            jnp.concatenate([w_query, w_key, w_value], axis=1),
            adapter_down.reshape(-1, weight_width),
            adapter_up_query.reshape(-1, weight_width),
            adapter_up_value.reshape(-1, weight_width),
        ]
        bounds = [0]
        for piece in pieces:
            bounds.append(bounds[-1] + piece.shape[0])
        packed = lax.all_gather(jnp.concatenate(pieces, axis=0), "col", axis=0)
        weights = packed[:, : bounds[1]].reshape(-1, weight_width)
        down_local = packed[:, bounds[1] : bounds[2]].reshape((adapter_count,) + down_shape)
        up_query = packed[:, bounds[2] : bounds[3]].reshape(adapter_count, rank_width, -1)
        up_value = packed[:, bounds[3] : bounds[4]].reshape(adapter_count, rank_width, -1)
    with jax.named_scope("lowrank"):
        onehot = chosen[:, None] == jnp.arange(adapter_count, dtype=jnp.int32)[None, :]
        partial_all = jnp.einsum(
            "tf,sfr->tsr", hidden, down_local, preferred_element_type=jnp.float32
        )
        partial = jnp.sum(jnp.where(onehot[:, :, None], partial_all, 0.0), axis=1)
        distance = 1
        while distance < row_size:
            pairs = [(i, i ^ distance) for i in range(row_size)]
            partial = partial + lax.ppermute(partial, "row", pairs)
            distance *= 2
        lowrank = partial.astype(jnp.bfloat16)
        onehot_b = onehot.astype(jnp.bfloat16)
        spread_query = (onehot_b[:, :, None] * lowrank[:, None, :rank_width]).reshape(
            -1, adapter_count * rank_width
        )
        spread_value = (onehot_b[:, :, None] * lowrank[:, None, rank_width:]).reshape(
            -1, adapter_count * rank_width
        )
        delta_query = jnp.dot(
            spread_query,
            up_query.reshape(adapter_count * rank_width, -1),
            preferred_element_type=jnp.float32,
        )
        delta_value = jnp.dot(
            spread_value,
            up_value.reshape(adapter_count * rank_width, -1),
            preferred_element_type=jnp.float32,
        )
    with jax.named_scope("projection"):
        base = jnp.dot(full_rows, weights, preferred_element_type=jnp.float32)
        base_query = base[:, :query_width]
        base_key = base[:, query_width : query_width + key_width]
        base_value = base[:, query_width + key_width :]
    with jax.named_scope("rotary"):
        half_width = HEAD // 2
        frequency = jnp.exp(
            jnp.arange(half_width, dtype=jnp.float32) * (-2.0 * math.log(10000.0) / HEAD)
        )
        angles = position.astype(jnp.float32)[:, None] * frequency[None, :]
        cosine = jnp.cos(angles)[:, None, :]
        sine_value = jnp.sin(angles)[:, None, :]
        query = rotate(base_query + delta_query, cosine, sine_value).astype(jnp.bfloat16)
        key_rotated = rotate(base_key, cosine, sine_value).astype(jnp.bfloat16)
        value_rows = (base_value + delta_value).astype(jnp.bfloat16)
    with jax.named_scope("cache_write"):
        pages = page_table.shape[1]
        rows, keep = cache_rows(lengths, starts, page_table[0])
        key_cache = jnp.where(keep[:, None], jnp.take(key_rotated, rows, axis=0), 0).reshape(
            pages, PAGE, key_width
        )
        value_cache = jnp.where(keep[:, None], jnp.take(value_rows, rows, axis=0), 0).reshape(
            pages, PAGE, key_width
        )
    return (query, key_cache.astype(jnp.bfloat16), value_cache.astype(jnp.bfloat16))


def solution(mesh):
    return jax.shard_map(
        shards,
        mesh=mesh,
        in_specs=(
            P("col", "row"),
            P("col", "row"),
            P("col", "row"),
            P("col", "row"),
            P("col", "row", None),
            P("col", None, "row"),
            P("col", None, "row"),
            P("col", None),
            P("col", None),
            P(),
            P("col", None),
        ),
        out_specs=(P("col", "row"), P("col", None, "row"), P("col", None, "row")),
        check_vma=False,
    )
```

profile of v0, /device:TPU:1, one launch (start us, length us, event | category | flops | bytes accessed | tf_op | source)
XLA Modules:
  0.0 240.4 jit_solution(12034622873768710716)
XLA Ops:
  7.3 0.7 reshape.325
  8.0 0.7 reshape.324
  8.7 0.9 copy.31
  9.8 1.8 maximum_bitcast_fusion
  11.7 0.7 all-gather.5.cloned.1.call-update
  12.8 0.7 gather_fusion
  13.8 0.7 compare_and_fusion
  14.5 0.7 fusion.10
  15.2 1.0 multiply_cosine_fusion
  16.2 112.1 %all-gather.7.cloned.1.call-done = bf16[32,174,1024]{2,1,0:T(8,128)(2,1)} async-done(((bf16[1,174,1024]{2,1,0:T(8,128)(2,1)}), bf16[32,174,1024]{2,1,0:T(8,128)(2,1)}) %all-gather.7.cloned.1.call-update) | async-done | bytes 11403280 | tf_op jit(solution)/shard_map/gathers/all_gather | solution.py:95
  128.3 1.4 slice-done.3
  129.7 4.8 %reshape.328 = bf16[32,576,32]{2,1,0:T(8,128)(2,1)} reshape(bf16[32,18,1024]{2,1,0:T(8,128)(2,1)S(1)} %slice-done.3) | data formatting | bytes 2359296 | tf_op jit(solution)/shard_map/gathers/reshape | solution.py:97
  134.6 5.6 %fusion = f32[1024,32]{0,1:T(8,128)S(1)} fusion(bf16[32,576,32]{2,1,0:T(8,128)(2,1)} %reshape.328, pred[1024,32]{0,1:T(8,128)(4,1)S(1)} %get-tuple-element.23, bf16[1024,576]{0,1:T(8,128)(2,1)S(1)} %copy-done.2), kind=kOutput, calls=%fused_computation.4 | convolution fusion | flops 1210023936 | bytes 2523136 | tf_op jit(solution)/shard_map/lowrank/tf,sfr->tsr/dot_general | solution.py:102
  140.1 1.5 collective-permute-start
  141.6 0.6 fusion.4
  142.3 9.5 %slice.58 = bf16[32,144,1024]{2,1,0:T(8,128)(2,1)} slice(bf16[32,174,1024]{2,1,0:T(8,128)(2,1)} %all-gather.7.cloned.1.call-done), slice={[0:32], [0:144], [0:1024]} | slice | bytes 18874368 | tf_op jit(solution)/shard_map/gathers/slice | solution.py:96
  151.8 1.6 collective-permute-start.1
  153.4 33.7 %all-gather.5.cloned.1.call-done = bf16[1024,4608]{0,1:T(8,128)(2,1)} async-done(((bf16[1024,576]{0,1:T(8,128)(2,1)}), bf16[1024,4608]{0,1:T(8,128)(2,1)}) %all-gather.5.cloned.1.call-update) | async-done | bytes 9437200 | tf_op jit(solution)/shard_map/gathers/all_gather | solution.py:85
  187.1 14.7 %convolution_bitcast_fusion = f32[1024,1024]{0,1:T(8,128)S(1)} fusion(bf16[4608,1024]{1,0:T(8,128)(2,1)} %bitcast.63, bf16[1024,4608]{0,1:T(8,128)(2,1)} %all-gather.5.cloned.1.call-done), kind=kOutput, calls=%fused_computation.5 | convolution fusion | flops 9663676416 | bytes 23068672 | tf_op jit(solution)/shard_map/projection/dot_general | solution.py:130
  201.9 2.7 %collective-permute-start.2 = (f32[1024,32]{0,1:T(8,128)S(1)}, f32[1024,32]{0,1:T(8,128)S(1)}, u32[]{:S(2)}, u32[]{:S(2)}) collective-permute-start(f32[1024,32]{0,1:T(8,128)S(1)} %add.98), channel_id=1, source_target_pairs={{0,128},{32,160},{64,192},{96,224},{128,0},{160,32},{192,64},{224,... | collective-permute-start | bytes 393224 | tf_op jit(solution)/shard_map/lowrank/ppermute | solution.py:109
  205.2 1.4 slice.62
  206.6 1.0 reshape.329
  207.6 0.2 copy.40
  207.8 6.9 %gather_fusion.1 = bf16[2304,256]{1,0:T(8,128)(2,1)S(1)} fusion(bf16[1024,256]{1,0:T(8,128)(2,1)S(1)} %copy.40, s32[3072]{0:T(1024)S(1)} %pad_clamp_fusion), kind=kCustom, calls=%fused_computation.clone | custom fusion | bytes 2368512 | tf_op jit(solution)/shard_map/cache_write/jit(_take)/gather | solution.py:148
  214.7 1.0 broadcast_multiply_fusion
  215.7 2.5 %fusion.1 = bf16[1024,256]{0,1:T(8,128)(2,1)} fusion(bf16[1024,512]{0,1:T(8,128)(2,1)S(1)} %bitcast.68, bf16[512,256]{1,0:T(8,128)(2,1)S(1)} %reshape.333, f32[1024,1024]{0,1:T(8,128)} %copy-done.1), kind=kOutput, calls=%fused_computation.8 | convolution fusion | flops 268959744 | bytes 2883584 | tf_op jit(solution)/shard_map/lowrank/dot_general | solution.py:124
  218.2 1.2 copy.36
  219.5 2.5 %slice_add_fusion = f32[1024,512]{0,1:T(8,128)S(1)} fusion(f32[1024,1024]{0,1:T(8,128)} %copy-done.1, bf16[1024,512]{0,1:T(8,128)(2,1)S(1)} %bitcast.67, bf16[512,512]{1,0:T(8,128)(2,1)} %reshape.329), kind=kOutput, calls=%fused_computation.6 | convolution fusion | flops 537395200 | bytes 5767168 | tf_op jit(solution)/shard_map/lowrank/dot_general | solution.py:119
  222.0 0.3 subtract_convert_fusion
  222.5 1.3 copy.39
  223.8 6.9 %gather_fusion.2 = bf16[2304,256]{1,0:T(8,128)(2,1)S(1)} fusion(bf16[1024,256]{1,0:T(8,128)(2,1)S(1)} %copy.36, s32[3072]{0:T(1024)S(1)} %pad_clamp_fusion), kind=kCustom, calls=%fused_computation.1.clone | custom fusion | bytes 2368512 | tf_op jit(solution)/shard_map/cache_write/jit(_take)/gather | solution.py:151
  230.7 2.9 %select_select_fusion = (bf16[2304,256]{1,0:T(8,128)(2,1)}, bf16[2304,256]{1,0:T(8,128)(2,1)}) fusion(bf16[2304,256]{1,0:T(8,128)(2,1)S(1)} %gather_fusion.2, pred[2304]{0:T(1024)(128)(4,1)S(1)} %copy-done.3, pred[2304]{0:T(1024)(128)(4,1)S(1)} %copy-done.4, bf16[2304,256]{1,0:T(8,128)(2,1)S(1)} %gather_fusion.1), kind=kLoop, calls=%fused_computation.10 | loop fusion | flops 2359296 | bytes 4723200 | tf_op jit(solution)/shard_map/cache_write/jit(_where)/select_n | solution.py:151
  (55 shorter events, 1.9 us)
Async XLA Ops:
  7.2 5.6 %copy-start = (s32[32]{0:T(128)S(1)}, s32[32]{0:T(128)}, u32[]{:S(2)}) copy-start(s32[32]{0:T(128)} %param.22) | copy-start | bytes 388
  7.2 5.2 %copy-start.5 = (s32[1,10]{1,0:T(1,128)S(1)}, s32[1,10]{1,0:T(1,128)}, u32[]{:S(2)}) copy-start(s32[1,10]{1,0:T(1,128)} %param.20) | copy-start | bytes 124
  7.2 5.6 %copy-start.6 = (s32[1,10]{1,0:T(1,128)S(1)}, s32[1,10]{1,0:T(1,128)}, u32[]{:S(2)}) copy-start(s32[1,10]{1,0:T(1,128)} %param.21) | copy-start | bytes 124
  7.2 6.2 %copy-start.7 = (s32[1,18]{1,0:T(1,128)S(1)}, s32[1,18]{1,0:T(1,128)}, u32[]{:S(2)}) copy-start(s32[1,18]{1,0:T(1,128)} %param.23) | copy-start | bytes 220
  7.2 121.1 %all-gather.7.cloned.1.call-start = ((), (), s32[]{:S(2)}) async-start(), calls=%async_computation.1 | async-start | bytes 11894784 | tf_op jit(solution)/shard_map/gathers/all_gather | solution.py:95
  11.6 175.5 %all-gather.5.cloned.1.call-start = ((), (), s32[]{:S(2)}) async-start(), calls=%async_computation | async-start | bytes 10616832 | tf_op jit(solution)/shard_map/gathers/all_gather | solution.py:85
  128.3 1.4 slice-start.3
  129.7 4.9 %copy-start.2 = (bf16[1024,576]{0,1:T(8,128)(2,1)S(1)}, bf16[1024,576]{0,1:T(8,128)(2,1)}, u32[]{:S(2)}) copy-start(bf16[1024,576]{0,1:T(8,128)(2,1)} %param.13) | copy-start | bytes 3538948
  140.1 11.7 %collective-permute-start = (f32[1024,32]{0,1:T(8,128)S(1)}, f32[1024,32]{0,1:T(8,128)S(1)}, u32[]{:S(2)}, u32[]{:S(2)}) collective-permute-start(f32[1024,32]{0,1:T(8,128)S(1)} %fusion), channel_id=1, source_target_pairs={{0,32},{32,0},{64,96},{96,64},{128,160},{160,128},{192,224},{224,1... | collective-permute-start | bytes 393224 | tf_op jit(solution)/shard_map/lowrank/ppermute | solution.py:109
  151.8 50.1 %collective-permute-start.1 = (f32[1024,32]{0,1:T(8,128)S(1)}, f32[1024,32]{0,1:T(8,128)S(1)}, u32[]{:S(2)}, u32[]{:S(2)}) collective-permute-start(f32[1024,32]{0,1:T(8,128)S(1)} %add.97), channel_id=1, source_target_pairs={{0,64},{32,96},{64,0},{96,32},{128,192},{160,224},{192,128},{224,1... | collective-permute-start | bytes 393224 | tf_op jit(solution)/shard_map/lowrank/ppermute | solution.py:109
  187.1 17.7 %slice-start = ((s8[11534336]{0:T(1024)(128)(4,1)}), s8[4194304]{0:T(1024)(128)(4,1)S(1)}, s32[]{:S(2)}) async-start(s8[11534336]{0:T(1024)(128)(4,1)} %bitcast.61), calls=%async_computation.2 | async-start | bytes 8388608
  187.1 17.7 %slice-start.1 = ((s8[11534336]{0:T(1024)(128)(4,1)}), s8[4194304]{0:T(1024)(128)(4,1)S(1)}, s32[]{:S(2)}) async-start(s8[11534336]{0:T(1024)(128)(4,1)} %bitcast.61), calls=%async_computation.3 | async-start | bytes 8388608
  187.1 17.8 %slice-start.2 = ((s8[11534336]{0:T(1024)(128)(4,1)}), s8[3145728]{0:T(1024)(128)(4,1)S(1)}, s32[]{:S(2)}) async-start(s8[11534336]{0:T(1024)(128)(4,1)} %bitcast.61), calls=%async_computation.4 | async-start | bytes 6291456
  201.8 3.0 %copy-start.1 = (f32[1024,1024]{0,1:T(8,128)}, f32[1024,1024]{0,1:T(8,128)S(1)}, u32[]{:S(2)}) copy-start(f32[1024,1024]{0,1:T(8,128)S(1)} %convolution_bitcast_fusion) | copy-start | bytes 12582916
  201.9 12.8 %collective-permute-start.2 = (f32[1024,32]{0,1:T(8,128)S(1)}, f32[1024,32]{0,1:T(8,128)S(1)}, u32[]{:S(2)}, u32[]{:S(2)}) collective-permute-start(f32[1024,32]{0,1:T(8,128)S(1)} %add.98), channel_id=1, source_target_pairs={{0,128},{32,160},{64,192},{96,224},{128,0},{160,32},{192,64},{224,... | collective-permute-start | bytes 393224 | tf_op jit(solution)/shard_map/lowrank/ppermute | solution.py:109
  223.8 6.9 %copy-start.3 = (pred[2304]{0:T(1024)(128)(4,1)S(1)}, pred[2304]{0:T(1024)(128)(4,1)}, u32[]{:S(2)}) copy-start(pred[2304]{0:T(1024)(128)(4,1)} %compare_and_fusion) | copy-start | bytes 6916
  223.8 6.9 %copy-start.4 = (pred[2304]{0:T(1024)(128)(4,1)S(1)}, pred[2304]{0:T(1024)(128)(4,1)}, u32[]{:S(2)}) copy-start(pred[2304]{0:T(1024)(128)(4,1)} %fusion.4) | copy-start | bytes 6916
Sparse Core Ops, SparseCore 0:
  11.7 116.5 all-gather.6
  130.1 56.9 all-gather.4
where the time goes:
time: 241 us; the launch traced here: 240 us
  waiting for transfers between devices  147 us (61%)
  local copies, waits for them, and re-layouts  38.3 us (16%)
  matrix products  25.3 us (10%)
  between operations  14.4 us (6%)
  other arithmetic  10 us (4%)
  starting transfers between devices  5.83 us (2%)
    all_gather x1, waiting for transfers between devices, shards(): packed = lax.all_gather(jnp.concatenate(pieces, axis=0), 'col', axis=0)  112 us
    all_gather x1, waiting for transfers between devices, shards(): full_rows = lax.all_gather(hidden, 'row', axis=1, tiled=True)  33.7 us
    dot_general x1, matrix products, shards(): base = jnp.dot(full_rows, weights, preferred_element_type=jnp.float32)  14.7 us
    slice x1, local copies, waits for them, and re-layouts, shards(): weights = packed[:, :bounds[1]].reshape(-1, weight_width)  9.52 us
    gather x1, local copies, waits for them, and re-layouts, shards(): jnp.take(key_rotated, rows, axis=0)  6.86 us
    gather x1, local copies, waits for them, and re-layouts, shards(): jnp.take(value_rows, rows, axis=0)  6.86 us
    ppermute x3, starting transfers between devices, shards(): partial = partial + lax.ppermute(partial, 'row', pairs)  5.75 us
    dot_general x1, matrix products, shards(): jnp.einsum('tf,sfr->tsr', hidden, down_local, preferred_element_type=jnp....  5.55 us
  transfers between devices with their start and end apart: 5, of which 2 were waited for; matrix products, arithmetic and copies ran while one was open for 20% of the time, Pallas kernels for 0%

commit v1 on v0

--- a/solution.py
+++ b/solution.py
@@ -7,6 +7,22 @@
 HEAD = 128
 PAGE = 128
 TOK_DEV = 1024
+
+
+def collect(x, axis, dim):
+    ways, here, turn = (lax.axis_size(axis), lax.axis_index(axis), x.shape[dim])
+    shape = [n * ways if d == dim else n for d, n in enumerate(x.shape)]
+    full = lax.dynamic_update_slice_in_dim(jnp.zeros(shape, x.dtype), x, here * turn, axis=dim)
+    going_up = going_down = x
+    for far in range(1, ways // 2 + 1):
+        going_up = lax.ppermute(going_up, axis, [(d, (d + 1) % ways) for d in range(ways)])
+        full = lax.dynamic_update_slice_in_dim(full, going_up, (here - far) % ways * turn, axis=dim)
+        if 2 * far < ways:
+            going_down = lax.ppermute(going_down, axis, [(d, (d - 1) % ways) for d in range(ways)])
+            full = lax.dynamic_update_slice_in_dim(
+                full, going_down, (here + far) % ways * turn, axis=dim
+            )
+    return full
 
 
 def rotate(values, cosine, sine_value):
@@ -82,7 +98,7 @@
     down_shape = adapter_down.shape[1:]
     row_size = lax.axis_size("row")
     with jax.named_scope("gathers"):
-        full_rows = lax.all_gather(hidden, "row", axis=1, tiled=True)
+        full_rows = collect(hidden, "row", 1)
         pieces = [
             jnp.concatenate([w_query, w_key, w_value], axis=1),
             adapter_down.reshape(-1, weight_width),

time: 241 us -> 216 us (0.90)
  waiting for transfers between devices: 147 us -> 75.3 us
  local copies, waits for them, and re-layouts: 38.3 us -> 61 us
  starting transfers between devices: 5.83 us -> 20.8 us
  other arithmetic: 10 us -> 16.4 us
    all_gather x1, waiting for transfers between devices: 112 us -> 55.6 us  [shards(): packed = lax.all_gather(jnp.concatenate(pieces, axis=0), 'col', axis=0)]
    all_gather x1 -> x0, waiting for transfers between devices: 33.7 us -> none  [shards(): full_rows = lax.all_gather(hidden, 'row', axis=1, tiled=True)]
    ppermute x0 -> x7, waiting for transfers between devices: none -> 19.6 us  [the longest x4 19.6 us: collect(): lax.ppermute(going_up, axis, [(d, (d + 1) % ways) for d in range(ways)])]
    dynamic_update_slice x0 -> x8, local copies, waits for them, and re-layouts: none -> 16.7 us  [the longest x4 8.26 us: collect(): lax.dynamic_update_slice_in_dim(full, going_up, (here - far) % ways * tur...]
    ppermute x0 -> x7, starting transfers between devices: none -> 15.5 us  [the longest x4 10.1 us: collect(): lax.ppermute(going_up, axis, [(d, (d + 1) % ways) for d in range(ways)])]
    broadcast_in_dim x0 -> x1, local copies, waits for them, and re-layouts: none -> 4.86 us  [collect(): jnp.zeros(shape, x.dtype)]
  transfers between devices with their start and end apart: 5 -> 11, of which waited for: 2 -> 4; matrix products, arithmetic and copies ran while one was open for 20% -> 33% of each run, Pallas kernels for 0% -> 0%
where the time goes in v1:
time: 216 us; the launch traced here: 215 us
  waiting for transfers between devices  75.3 us (35%)
  local copies, waits for them, and re-layouts  61 us (28%)
  matrix products  27 us (12%)
  starting transfers between devices  20.8 us (10%)
  other arithmetic  16.4 us (8%)
  between operations  14.3 us (7%)
    all_gather x1, waiting for transfers between devices, shards(): packed = lax.all_gather(jnp.concatenate(pieces, axis=0), 'col', axis=0)  55.6 us
    ppermute x4, waiting for transfers between devices, collect(): lax.ppermute(going_up, axis, [(d, (d + 1) % ways) for d in range(ways)])  19.6 us
    dot_general x1, matrix products, shards(): base = jnp.dot(full_rows, weights, preferred_element_type=jnp.float32)  16 us
    ppermute x4, starting transfers between devices, collect(): lax.ppermute(going_up, axis, [(d, (d + 1) % ways) for d in range(ways)])  10.1 us
    slice x1, local copies, waits for them, and re-layouts, shards(): weights = packed[:, :bounds[1]].reshape(-1, weight_width)  9.15 us
    dynamic_update_slice x4, local copies, waits for them, and re-layouts, collect(): lax.dynamic_update_slice_in_dim(full, going_up, (here - far) % ways * tur...  8.26 us
    dynamic_update_slice x3, local copies, waits for them, and re-layouts, collect(): lax.dynamic_update_slice_in_dim(full, going_down, (here + far) % ways * t...  7.33 us
    gather x1, local copies, waits for them, and re-layouts, shards(): jnp.take(value_rows, rows, axis=0)  6.86 us
  transfers between devices with their start and end apart: 11, of which 4 were waited for; matrix products, arithmetic and copies ran while one was open for 33% of the time, Pallas kernels for 0%

profile of v1, /device:TPU:1, one launch (start us, length us, event | category | flops | bytes accessed | tf_op | source)
XLA Modules:
  0.0 214.7 jit_solution(13144931657229541507)
XLA Ops:
  9.8 1.8 maximum_bitcast_fusion
  11.6 2.7 %collective-permute-start = (bf16[1024,576]{0,1:T(8,128)(2,1)}, bf16[1024,576]{0,1:T(8,128)(2,1)S(1)}, u32[]{:S(2)}, u32[]{:S(2)}) collective-permute-start(bf16[1024,576]{0,1:T(8,128)(2,1)} %param.13), channel_id=1, source_target_pairs={{0,32},{32,64},{64,96},{96,128},{128,160},{160,192},{192,224},{224... | collective-permute-start | bytes 3538952 | tf_op jit(solution)/shard_map/gathers/ppermute | solution.py:18
  16.9 10.8 %collective-permute-done = bf16[1024,576]{0,1:T(8,128)(2,1)S(1)} collective-permute-done((bf16[1024,576]{0,1:T(8,128)(2,1)}, bf16[1024,576]{0,1:T(8,128)(2,1)S(1)}, u32[]{:S(2)}, u32[]{:S(2)}) %collective-permute-start) | collective-permute-done | bytes 1179680 | tf_op jit(solution)/shard_map/gathers/ppermute | solution.py:18
  27.7 2.4 %collective-permute-start.2 = (bf16[1024,576]{0,1:T(8,128)(2,1)S(1)}, bf16[1024,576]{0,1:T(8,128)(2,1)}, u32[]{:S(2)}, u32[]{:S(2)}) collective-permute-start(bf16[1024,576]{0,1:T(8,128)(2,1)S(1)} %collective-permute-done), channel_id=1, source_target_pairs={{0,32},{32,64},{64,96},{96,128},{128,160},{160,192},{192,224},{224... | collective-permute-start | bytes 3538952 | tf_op jit(solution)/shard_map/gathers/ppermute | solution.py:18
  34.6 1.7 collective-permute-start.3
  36.4 6.8 %collective-permute-done.2 = bf16[1024,576]{0,1:T(8,128)(2,1)} collective-permute-done((bf16[1024,576]{0,1:T(8,128)(2,1)S(1)}, bf16[1024,576]{0,1:T(8,128)(2,1)}, u32[]{:S(2)}, u32[]{:S(2)}) %collective-permute-start.2) | collective-permute-done | bytes 1179680 | tf_op jit(solution)/shard_map/gathers/ppermute | solution.py:18
  43.3 2.6 %collective-permute-start.4 = (bf16[1024,576]{0,1:T(8,128)(2,1)}, bf16[1024,576]{0,1:T(8,128)(2,1)}, u32[]{:S(2)}, u32[]{:S(2)}) collective-permute-start(bf16[1024,576]{0,1:T(8,128)(2,1)} %collective-permute-done.2), channel_id=1, source_target_pairs={{0,32},{32,64},{64,96},{96,128},{128,160},{160,192},{192,224},{224... | collective-permute-start | bytes 3538952 | tf_op jit(solution)/shard_map/gathers/ppermute | solution.py:18
  45.8 4.9 %broadcast_in_dim.35 = bf16[1024,4608]{0,1:T(8,128)(2,1)} broadcast(bf16[]{:T(256)} %constant.104.clone.1), dimensions={} | broadcast | bytes 9437186 | tf_op jit(solution)/shard_map/gathers/broadcast_in_dim | solution.py:15
  52.6 1.7 multiply_cosine_fusion
  54.3 3.1 %collective-permute-start.5 = (bf16[1024,576]{0,1:T(8,128)(2,1)}, bf16[1024,576]{0,1:T(8,128)(2,1)}, u32[]{:S(2)}, u32[]{:S(2)}) collective-permute-start(bf16[1024,576]{0,1:T(8,128)(2,1)} %collective-permute-done.3), channel_id=1, source_target_pairs={{0,224},{32,0},{64,32},{96,64},{128,96},{160,128},{192,160},{224,1... | collective-permute-start | bytes 3538952 | tf_op jit(solution)/shard_map/gathers/ppermute | solution.py:21
  57.4 1.9 collective-permute-done.4
  59.3 2.5 %collective-permute-start.6 = (bf16[1024,576]{0,1:T(8,128)(2,1)}, bf16[1024,576]{0,1:T(8,128)(2,1)}, u32[]{:S(2)}, u32[]{:S(2)}) collective-permute-start(bf16[1024,576]{0,1:T(8,128)(2,1)} %collective-permute-done.4), channel_id=1, source_target_pairs={{0,32},{32,64},{64,96},{96,128},{128,160},{160,192},{192,224},{224... | collective-permute-start | bytes 3538952 | tf_op jit(solution)/shard_map/gathers/ppermute | solution.py:18
  62.9 2.4 %constant_dynamic-update-slice_fusion.5 = bf16[1024,4608]{0,1:T(8,128)(2,1)} fusion(bf16[1024,4608]{0,1:T(8,128)(2,1)} %constant_dynamic-update-slice_fusion.6, bf16[1024,576]{0,1:T(8,128)(2,1)} %collective-permute-done.1, s32[]{:T(128)S(6)} %select_n.121), kind=kLoop, calls=%fused_computation.50 | loop fusion | bytes 2359300 | tf_op jit(solution)/shard_map/gathers/dynamic_update_slice | solution.py:22
  65.2 2.4 %constant_dynamic-update-slice_fusion.4 = bf16[1024,4608]{0,1:T(8,128)(2,1)} fusion(bf16[1024,4608]{0,1:T(8,128)(2,1)} %constant_dynamic-update-slice_fusion.5, bf16[1024,576]{0,1:T(8,128)(2,1)} %collective-permute-done.2, s32[]{:T(128)S(6)} %select_n.123), kind=kLoop, calls=%fused_computation.49 | loop fusion | bytes 2359300 | tf_op jit(solution)/shard_map/gathers/dynamic_update_slice | solution.py:19
  67.7 2.6 %constant_dynamic-update-slice_fusion.3 = bf16[1024,4608]{0,1:T(8,128)(2,1)} fusion(bf16[1024,4608]{0,1:T(8,128)(2,1)} %constant_dynamic-update-slice_fusion.4, bf16[1024,576]{0,1:T(8,128)(2,1)} %collective-permute-done.3, s32[]{:T(128)S(6)} %select_n.125), kind=kLoop, calls=%fused_computation.48 | loop fusion | bytes 2359300 | tf_op jit(solution)/shard_map/gathers/dynamic_update_slice | solution.py:22
  70.3 2.4 %constant_dynamic-update-slice_fusion.2 = bf16[1024,4608]{0,1:T(8,128)(2,1)} fusion(bf16[1024,4608]{0,1:T(8,128)(2,1)} %constant_dynamic-update-slice_fusion.3, bf16[1024,576]{0,1:T(8,128)(2,1)} %collective-permute-done.4, s32[]{:T(128)S(6)} %select_n.127), kind=kLoop, calls=%fused_computation.47 | loop fusion | bytes 2359300 | tf_op jit(solution)/shard_map/gathers/dynamic_update_slice | solution.py:19
  72.6 55.6 %all-gather.4.cloned.1.call-done = bf16[32,174,1024]{2,1,0:T(8,128)(2,1)} async-done(((bf16[1,174,1024]{2,1,0:T(8,128)(2,1)}), bf16[32,174,1024]{2,1,0:T(8,128)(2,1)}) %all-gather.4.cloned.1.call-update) | async-done | bytes 11403280 | tf_op jit(solution)/shard_map/gathers/all_gather | solution.py:111
  128.3 1.4 slice-done.3
  129.7 4.8 %reshape.328 = bf16[32,576,32]{2,1,0:T(8,128)(2,1)} reshape(bf16[32,18,1024]{2,1,0:T(8,128)(2,1)S(1)} %slice-done.3) | data formatting | bytes 2359296 | tf_op jit(solution)/shard_map/gathers/reshape | solution.py:113
  134.5 5.5 %fusion = f32[1024,32]{0,1:T(8,128)S(1)} fusion(bf16[32,576,32]{2,1,0:T(8,128)(2,1)} %reshape.328, pred[1024,32]{0,1:T(8,128)(4,1)S(1)} %get-tuple-element.25, bf16[1024,576]{0,1:T(8,128)(2,1)S(1)} %copy-done.4), kind=kOutput, calls=%fused_computation.4 | convolution fusion | flops 1210023936 | bytes 2523136 | tf_op jit(solution)/shard_map/lowrank/tf,sfr->tsr/dot_general | solution.py:118
  140.0 1.5 collective-permute-start.7
  141.5 2.4 %constant_dynamic-update-slice_fusion.1 = bf16[1024,4608]{0,1:T(8,128)(2,1)} fusion(bf16[1024,4608]{0,1:T(8,128)(2,1)} %constant_dynamic-update-slice_fusion.2, bf16[1024,576]{0,1:T(8,128)(2,1)} %collective-permute-done.5, s32[]{:T(128)S(6)} %select_n.129), kind=kLoop, calls=%fused_computation.46 | loop fusion | bytes 2359300 | tf_op jit(solution)/shard_map/gathers/dynamic_update_slice | solution.py:22
  145.2 2.4 %constant_dynamic-update-slice_fusion = bf16[1024,4608]{0,1:T(8,128)(2,1)} fusion(bf16[1024,4608]{0,1:T(8,128)(2,1)} %constant_dynamic-update-slice_fusion.1, bf16[1024,576]{0,1:T(8,128)(2,1)} %collective-permute-done.6, s32[]{:T(128)S(6)} %select_n.131), kind=kLoop, calls=%fused_computation.45 | loop fusion | bytes 2359300 | tf_op jit(solution)/shard_map/gathers/dynamic_update_slice | solution.py:19
  147.6 9.2 %slice.58 = bf16[32,144,1024]{2,1,0:T(8,128)(2,1)} slice(bf16[32,174,1024]{2,1,0:T(8,128)(2,1)} %all-gather.4.cloned.1.call-done), slice={[0:32], [0:144], [0:1024]} | slice | bytes 18874368 | tf_op jit(solution)/shard_map/gathers/slice | solution.py:112
  156.7 1.6 add.175
  158.3 2.5 %collective-permute-start.9 = (f32[1024,32]{0,1:T(8,128)}, f32[1024,32]{0,1:T(8,128)}, u32[]{:S(2)}, u32[]{:S(2)}) collective-permute-start(f32[1024,32]{0,1:T(8,128)} %add.175), channel_id=1, source_target_pairs={{0,128},{32,160},{64,192},{96,224},{128,0},{160,32},{192,64},{224,... | collective-permute-start | bytes 393224 | tf_op jit(solution)/shard_map/lowrank/ppermute | solution.py:125
  160.8 16.0 %fusion.12 = f32[1024,1024]{0,1:T(8,128)} fusion(bf16[1024,4608]{0,1:T(8,128)(2,1)} %constant_dynamic-update-slice_fusion, bf16[4608,1024]{1,0:T(8,128)(2,1)} %bitcast.61), kind=kOutput, calls=%fused_computation.74 | convolution fusion | flops 9663676416 | bytes 23068672 | tf_op jit(solution)/shard_map/projection/dot_general | solution.py:146
  182.3 2.4 %slice_add_fusion = f32[1024,512]{0,1:T(8,128)S(1)} fusion(f32[1024,1024]{0,1:T(8,128)} %fusion.12, bf16[1024,512]{0,1:T(8,128)(2,1)S(1)} %bitcast.66, bf16[512,512]{1,0:T(8,128)(2,1)S(1)} %reshape.329), kind=kOutput, calls=%fused_computation.5 | convolution fusion | flops 537395200 | bytes 5767168 | tf_op jit(solution)/shard_map/lowrank/dot_general | solution.py:135
  186.5 3.0 %fusion.2 = (bf16[1024,256]{0,1:T(8,128)(2,1)}, f32[1024,256]{0,1:T(8,128)S(1)}) fusion(f32[1024,1024]{0,1:T(8,128)} %fusion.12, bf16[1024,512]{0,1:T(8,128)(2,1)S(1)} %bitcast.64, bf16[512,256]{1,0:T(8,128)(2,1)} %reshape.333), kind=kOutput, calls=%fused_computation.10 | convolution fusion | flops 268959744 | bytes 4980736 | tf_op jit(solution)/shard_map/lowrank/dot_general | solution.py:140
  191.2 6.9 %gather_fusion.2 = bf16[2304,256]{1,0:T(8,128)(2,1)S(1)} fusion(bf16[1024,256]{1,0:T(8,128)(2,1)S(1)} %copy.36, s32[3072]{0:T(1024)S(1)} %pad_clamp_fusion), kind=kCustom, calls=%fused_computation.1.clone | custom fusion | bytes 2368512 | tf_op jit(solution)/shard_map/cache_write/jit(_take)/gather | solution.py:167
  198.1 6.9 %gather_fusion.1 = bf16[2304,256]{1,0:T(8,128)(2,1)S(1)} fusion(bf16[1024,256]{1,0:T(8,128)(2,1)S(1)} %copy.40, s32[3072]{0:T(1024)S(1)} %pad_clamp_fusion), kind=kCustom, calls=%fused_computation.clone | custom fusion | bytes 2368512 | tf_op jit(solution)/shard_map/cache_write/jit(_take)/gather | solution.py:164
  205.0 2.9 %select_select_fusion = (bf16[2304,256]{1,0:T(8,128)(2,1)}, bf16[2304,256]{1,0:T(8,128)(2,1)}) fusion(bf16[2304,256]{1,0:T(8,128)(2,1)S(1)} %gather_fusion.2, pred[2304]{0:T(1024)(128)(4,1)S(1)} %copy-done.6, pred[2304]{0:T(1024)(128)(4,1)S(1)} %copy-done.7, bf16[2304,256]{1,0:T(8,128)(2,1)S(1)} %gather_fusion.1), kind=kLoop, calls=%fused_computation.7 | loop fusion | flops 2359296 | bytes 4723200 | tf_op jit(solution)/shard_map/cache_write/jit(_where)/select_n | solution.py:167
  (74 shorter events, 22.9 us)
Async XLA Ops:
  7.2 24.0 %copy-start = (s32[32]{0:T(128)S(1)}, s32[32]{0:T(128)}, u32[]{:S(2)}) copy-start(s32[32]{0:T(128)} %param.22) | copy-start | bytes 388
  7.2 121.1 %all-gather.4.cloned.1.call-start = ((), (), s32[]{:S(2)}) async-start(), calls=%async_computation | async-start | bytes 11894784 | tf_op jit(solution)/shard_map/gathers/all_gather | solution.py:111
  11.6 16.2 %collective-permute-start = (bf16[1024,576]{0,1:T(8,128)(2,1)}, bf16[1024,576]{0,1:T(8,128)(2,1)S(1)}, u32[]{:S(2)}, u32[]{:S(2)}) collective-permute-start(bf16[1024,576]{0,1:T(8,128)(2,1)} %param.13), channel_id=1, source_target_pairs={{0,32},{32,64},{64,96},{96,128},{128,160},{160,192},{192,224},{224... | collective-permute-start | bytes 3538952 | tf_op jit(solution)/shard_map/gathers/ppermute | solution.py:18
  14.3 20.3 %collective-permute-start.1 = (bf16[1024,576]{0,1:T(8,128)(2,1)}, bf16[1024,576]{0,1:T(8,128)(2,1)}, u32[]{:S(2)}, u32[]{:S(2)}) collective-permute-start(bf16[1024,576]{0,1:T(8,128)(2,1)} %param.13), channel_id=1, source_target_pairs={{0,224},{32,0},{64,32},{96,64},{128,96},{160,128},{192,160},{224,1... | collective-permute-start | bytes 3538952 | tf_op jit(solution)/shard_map/gathers/ppermute | solution.py:21
  27.7 15.5 %collective-permute-start.2 = (bf16[1024,576]{0,1:T(8,128)(2,1)S(1)}, bf16[1024,576]{0,1:T(8,128)(2,1)}, u32[]{:S(2)}, u32[]{:S(2)}) collective-permute-start(bf16[1024,576]{0,1:T(8,128)(2,1)S(1)} %collective-permute-done), channel_id=1, source_target_pairs={{0,32},{32,64},{64,96},{96,128},{128,160},{160,192},{192,224},{224... | collective-permute-start | bytes 3538952 | tf_op jit(solution)/shard_map/gathers/ppermute | solution.py:18
  34.6 19.7 %collective-permute-start.3 = (bf16[1024,576]{0,1:T(8,128)(2,1)}, bf16[1024,576]{0,1:T(8,128)(2,1)}, u32[]{:S(2)}, u32[]{:S(2)}) collective-permute-start(bf16[1024,576]{0,1:T(8,128)(2,1)} %collective-permute-done.1), channel_id=1, source_target_pairs={{0,224},{32,0},{64,32},{96,64},{128,96},{160,128},{192,160},{224,1... | collective-permute-start | bytes 3538952 | tf_op jit(solution)/shard_map/gathers/ppermute | solution.py:21
  43.3 16.0 %collective-permute-start.4 = (bf16[1024,576]{0,1:T(8,128)(2,1)}, bf16[1024,576]{0,1:T(8,128)(2,1)}, u32[]{:S(2)}, u32[]{:S(2)}) collective-permute-start(bf16[1024,576]{0,1:T(8,128)(2,1)} %collective-permute-done.2), channel_id=1, source_target_pairs={{0,32},{32,64},{64,96},{96,128},{128,160},{160,192},{192,224},{224... | collective-permute-start | bytes 3538952 | tf_op jit(solution)/shard_map/gathers/ppermute | solution.py:18
  45.8 4.9 %copy-start.4 = (bf16[1024,576]{0,1:T(8,128)(2,1)S(1)}, bf16[1024,576]{0,1:T(8,128)(2,1)}, u32[]{:S(2)}) copy-start(bf16[1024,576]{0,1:T(8,128)(2,1)} %param.13) | copy-start | bytes 3538948
  54.3 87.2 %collective-permute-start.5 = (bf16[1024,576]{0,1:T(8,128)(2,1)}, bf16[1024,576]{0,1:T(8,128)(2,1)}, u32[]{:S(2)}, u32[]{:S(2)}) collective-permute-start(bf16[1024,576]{0,1:T(8,128)(2,1)} %collective-permute-done.3), channel_id=1, source_target_pairs={{0,224},{32,0},{64,32},{96,64},{128,96},{160,128},{192,160},{224,1... | collective-permute-start | bytes 3538952 | tf_op jit(solution)/shard_map/gathers/ppermute | solution.py:21
  59.3 85.9 %collective-permute-start.6 = (bf16[1024,576]{0,1:T(8,128)(2,1)}, bf16[1024,576]{0,1:T(8,128)(2,1)}, u32[]{:S(2)}, u32[]{:S(2)}) collective-permute-start(bf16[1024,576]{0,1:T(8,128)(2,1)} %collective-permute-done.4), channel_id=1, source_target_pairs={{0,32},{32,64},{64,96},{96,128},{128,160},{160,192},{192,224},{224... | collective-permute-start | bytes 3538952 | tf_op jit(solution)/shard_map/gathers/ppermute | solution.py:18
  128.3 1.4 slice-start.3
  140.0 3.9 %collective-permute-start.7 = (f32[1024,32]{0,1:T(8,128)S(1)}, f32[1024,32]{0,1:T(8,128)S(1)}, u32[]{:S(2)}, u32[]{:S(2)}) collective-permute-start(f32[1024,32]{0,1:T(8,128)S(1)} %fusion), channel_id=1, source_target_pairs={{0,32},{32,0},{64,96},{96,64},{128,160},{160,128},{192,224},{224,1... | collective-permute-start | bytes 393224 | tf_op jit(solution)/shard_map/lowrank/ppermute | solution.py:125
  143.9 12.8 %collective-permute-start.8 = (f32[1024,32]{0,1:T(8,128)S(1)}, f32[1024,32]{0,1:T(8,128)}, u32[]{:S(2)}, u32[]{:S(2)}) collective-permute-start(f32[1024,32]{0,1:T(8,128)S(1)} %add.174), channel_id=1, source_target_pairs={{0,64},{32,96},{64,0},{96,32},{128,192},{160,224},{192,128},{224,1... | collective-permute-start | bytes 393224 | tf_op jit(solution)/shard_map/lowrank/ppermute | solution.py:125
  147.6 29.3 %slice-start = ((s8[11534336]{0:T(1024)(128)(4,1)}), s8[3145728]{0:T(1024)(128)(4,1)S(1)}, s32[]{:S(2)}) async-start(s8[11534336]{0:T(1024)(128)(4,1)} %bitcast.59), calls=%async_computation.1 | async-start | bytes 6291456
  158.3 22.8 %collective-permute-start.9 = (f32[1024,32]{0,1:T(8,128)}, f32[1024,32]{0,1:T(8,128)}, u32[]{:S(2)}, u32[]{:S(2)}) collective-permute-start(f32[1024,32]{0,1:T(8,128)} %add.175), channel_id=1, source_target_pairs={{0,128},{32,160},{64,192},{96,224},{128,0},{160,32},{192,64},{224,... | collective-permute-start | bytes 393224 | tf_op jit(solution)/shard_map/lowrank/ppermute | solution.py:125
  160.8 16.1 %slice-start.1 = ((s8[11534336]{0:T(1024)(128)(4,1)}), s8[4194304]{0:T(1024)(128)(4,1)S(1)}, s32[]{:S(2)}) async-start(s8[11534336]{0:T(1024)(128)(4,1)} %bitcast.59), calls=%async_computation.2 | async-start | bytes 8388608
  160.8 16.1 %slice-start.2 = ((s8[11534336]{0:T(1024)(128)(4,1)}), s8[4194304]{0:T(1024)(128)(4,1)S(1)}, s32[]{:S(2)}) async-start(s8[11534336]{0:T(1024)(128)(4,1)} %bitcast.59), calls=%async_computation.3 | async-start | bytes 8388608
  176.9 5.3 %copy-start.5 = (bf16[1024,32]{0,1:T(8,128)(2,1)S(1)}, bf16[1024,32]{0,1:T(8,128)(2,1)}, u32[]{:S(2)}) copy-start(bf16[1024,32]{0,1:T(8,128)(2,1)} %get-tuple-element.24) | copy-start | bytes 196612
  182.3 2.4 %copy-start.2 = (f32[1024,64]{0,1:T(8,128)S(1)}, f32[1024,64]{0,1:T(8,128)}, u32[]{:S(2)}) copy-start(f32[1024,64]{0,1:T(8,128)} %get-tuple-element.23) | copy-start | bytes 786436
  186.5 4.3 %copy-start.3 = (f32[1024,64]{0,1:T(8,128)S(1)}, f32[1024,64]{0,1:T(8,128)}, u32[]{:S(2)}) copy-start(f32[1024,64]{0,1:T(8,128)} %get-tuple-element.23) | copy-start | bytes 786436
  198.1 6.9 %copy-start.6 = (pred[2304]{0:T(1024)(128)(4,1)S(1)}, pred[2304]{0:T(1024)(128)(4,1)}, u32[]{:S(2)}) copy-start(pred[2304]{0:T(1024)(128)(4,1)} %compare_and_fusion) | copy-start | bytes 6916
  198.1 6.9 %copy-start.7 = (pred[2304]{0:T(1024)(128)(4,1)S(1)}, pred[2304]{0:T(1024)(128)(4,1)}, u32[]{:S(2)}) copy-start(pred[2304]{0:T(1024)(128)(4,1)} %fusion.4) | copy-start | bytes 6916
  198.1 9.8 %copy-start.1 = (s32[32]{0:T(128)S(1)}, s32[32]{0:T(128)}, u32[]{:S(2)}) copy-start(s32[32]{0:T(128)} %param.22) | copy-start | bytes 388
Sparse Core Ops, SparseCore 0:
  11.7 116.5 all-gather.3
